TPU v7x, 256 devices: a whole 4x4x8 slice. The times are simulated.
256 devices in a mesh: pipe: 2 (over core), seq: 4 (over x), tensor: 32 (over z, y).
Axes of the slice: x: 4, y: 4, z: 8, core: 2. Of those that a mesh axis runs over, the one named last changes fastest.
Arguments:
- token_ids: int32 [2, 768], P(None, 'seq'), may hold values from 0 to 511
- embed_table: bfloat16 [512, 8192], P(None, 'tensor'), may hold values from -24 to 24
- in_proj: bfloat16 [2, 8192, 3, 4096], P('pipe', None, None, 'tensor'), may hold values from -0.0625 to 0.0625
- feat_taps: float32 [2, 3, 3, 4096], P('pipe', None, None, 'tensor'), may hold values from -3 to 3
- se_taps: float32 [7, 4096], P(None, 'tensor'), may hold values from -2 to 2
- mr_taps: float32 [128, 4096], P(None, 'tensor'), may hold values from -0.6 to 0.6
- out_proj: bfloat16 [2, 4096, 8192], P('pipe', 'tensor'), may hold values from -0.1875 to 0.1875
- norm_gain: bfloat16 [2, 8192], P('pipe', 'tensor'), may hold values from 0.25 to 1.75
Outputs:
- segment_out: bfloat16 [2, 2, 768, 8192], P('pipe', None, 'seq', 'tensor')
All inputs are finite; a program needn't handle non-finite values.
Results may differ from a plain program's by a relative error of at most 0.023.
Values may be sent and summed in bfloat16 or wider, within the bound.
No kernel may reach another device: no remote copies, remote signals or barrier semaphores. Data moves between devices by JAX's collectives and lax.ppermute only.
A program may use at most 64 MiB of HBM per device.

v0:
```python
import jax
import jax.numpy as jnp
from jax import lax
from jax.sharding import PartitionSpec as P

VOCAB = 512
KL = 128
KS = 7
KF = 3
HALO = KL + KF - 2
epsilon = 1e-06


def swapped(value):
    return lax.ppermute(value, "pipe", [(0, 1), (1, 0)])


def of_section(core, own, other, section):
    return jnp.where(core == section, own, other)


def relaid_out_proj(w_down):
    n_t = lax.axis_size("tensor")
    chan_local, width = w_down.shape
    blocks = w_down.reshape(chan_local, n_t, width // n_t)
    moved = lax.all_to_all(blocks, "tensor", 1, 0, tiled=True)
    return moved.reshape(n_t * chan_local, width // n_t)


def section_step(x_in, w_in, feat, long_taps, w_out, gain):
    rows = x_in.shape[0]
    chan_local = w_in.shape[1] // 3
    aug = jnp.concatenate([x_in, gain.reshape(1, -1).astype(x_in.dtype)], axis=0)
    full = lax.all_gather(aug, "tensor", axis=1, tiled=True)
    values = full[:rows].astype(jnp.float32)
    gain_all = full[rows].astype(jnp.float32)
    inv_rms = lax.rsqrt(jnp.mean(values * values, axis=1, keepdims=True) + epsilon)
    normed = (values * inv_rms * gain_all[None, :]).astype(jnp.bfloat16)
    projected = jnp.dot(normed, w_in, preferred_element_type=jnp.float32).astype(jnp.bfloat16)
    blocks = lax.axis_size("pipe") * lax.axis_size("seq")
    kv_tail = projected[rows - HALO :, chan_local:]
    q_tail = projected[rows - (KF - 1) :, :chan_local]
    kv_prev, q_prev = lax.ppermute(
        (kv_tail, q_tail), ("pipe", "seq"), [(b, b + 1) for b in range(blocks - 1)]
    )
    q_all = jnp.concatenate([q_prev, projected[:, :chan_local]], axis=0).astype(jnp.float32)
    kv_all = jnp.concatenate([kv_prev, projected[:, chan_local:]], axis=0).astype(jnp.float32)
    q_taps = feat[:, 0, :]
    kv_taps = feat[:, 1:, :].reshape(KF, 2 * chan_local)
    kv_span = KL - 1 + rows
    q_feat = jnp.zeros((rows, chan_local), jnp.float32)
    kv_feat = jnp.zeros((kv_span, 2 * chan_local), jnp.float32)
    for tap_index in range(KF):
        offset = KF - 1 - tap_index
        q_feat = q_feat + q_taps[tap_index] * q_all[offset : offset + rows]
        kv_feat = kv_feat + kv_taps[tap_index] * kv_all[offset : offset + kv_span]
    gated_kv = kv_feat[:, :chan_local] * kv_feat[:, chan_local:]

    def add_tap(tap_index, running):
        shifted = lax.dynamic_slice_in_dim(gated_kv, KL - 1 - tap_index, rows, 0)
        return running + long_taps[tap_index] * shifted

    filtered = lax.fori_loop(0, KL, add_tap, jnp.zeros_like(q_feat))
    y_out = (q_feat * filtered).astype(jnp.bfloat16)
    y_full = lax.all_gather(y_out, "tensor", axis=1, tiled=True)
    mixed = jnp.dot(y_full, w_out, preferred_element_type=jnp.float32)
    return (x_in.astype(jnp.float32) + mixed).astype(jnp.bfloat16)


def local(token_ids, embed_table, in_proj, feat_taps, se_taps, mr_taps, out_proj, norm_gain):
    core = lax.axis_index("pipe")
    w_own = in_proj[0].reshape(in_proj.shape[1], -1)
    feat_own = feat_taps[0]
    gain_own = norm_gain[0]
    wt_own = relaid_out_proj(out_proj[0])
    w_other, feat_other, gain_other, wt_other = swapped((w_own, feat_own, gain_own, wt_own))
    padded_se = jnp.concatenate(
        [se_taps, jnp.zeros((KL - KS, se_taps.shape[1]), jnp.float32)], axis=0
    )
    filters = (padded_se, mr_taps)
    ids = lax.dynamic_index_in_dim(token_ids, core, 0, keepdims=False)
    vocab_ids = jnp.arange(VOCAB, dtype=jnp.int32)
    one_hot = (ids[:, None] == vocab_ids[None, :]).astype(jnp.bfloat16)
    current = jnp.dot(one_hot, embed_table, preferred_element_type=jnp.float32).astype(jnp.bfloat16)
    results = []
    for section in range(2):
        current = section_step(
            current,
            of_section(core, w_own, w_other, section),
            of_section(core, feat_own, feat_other, section),
            filters[section],
            of_section(core, wt_own, wt_other, section),
            of_section(core, gain_own, gain_other, section),
        )
        results.append(current)
    first_mine, second_mine = results
    second_slice_of_first = lax.ppermute(first_mine, "pipe", [(1, 0)])
    first_slice_of_second = lax.ppermute(second_mine, "pipe", [(0, 1)])
    lead = core == 0
    slice_zero = jnp.where(lead, first_mine, first_slice_of_second)
    slice_one = jnp.where(lead, second_slice_of_first, second_mine)
    return jnp.stack([slice_zero, slice_one], axis=0)[None]


def solution(mesh):
    return jax.shard_map(
        local,
        mesh=mesh,
        in_specs=(
            P(None, "seq"),
            P(None, "tensor"),
            P("pipe", None, None, "tensor"),
            P("pipe", None, None, "tensor"),
            P(None, "tensor"),
            P(None, "tensor"),
            P("pipe", "tensor", None),
            P("pipe", "tensor"),
        ),
        out_specs=P("pipe", None, "seq", "tensor"),
        check_vma=False,
    )
```

profile of v0, /device:TPU:1, one launch (start us, length us, event | category | flops | bytes accessed | tf_op | source)
XLA Modules:
  0.0 497.7 jit_solution(15193292453883227668)
XLA Ops:
  6.5 0.7 reduce
  7.3 3.3 collective-permute-start.1
  12.3 8.9 %copy.10 = bf16[1,8192,3,128]{1,3,2,0:T(8,128)(2,1)} copy(bf16[1,8192,3,128]{3,1,2,0:T(8,128)(2,1)} %param.14) | data formatting | bytes 12582912 | tf_op args[2]
  21.7 2.4 copy.11
  24.1 9.5 %all-to-all-start = ((bf16[128,32,256]{0,2,1:T(8,128)(2,1)}), bf16[128,32,256]{0,2,1:T(8,128)(2,1)S(1)}, u32[]{:S(2)}, u32[]{:S(2)}) async-start(bf16[128,32,256]{0,2,1:T(8,128)(2,1)} %bitcast.58), calls=%async_computation | async-start | bytes 4194304 | tf_op jit(solution)/shard_map/all_to_all | solution.py:26
  33.7 75.9 %all-gather.5.cloned.1.call-done = bf16[193,8192]{1,0:T(8,128)(2,1)} async-done(((bf16[193,256]{1,0:T(8,128)(2,1)}), bf16[193,8192]{1,0:T(8,128)(2,1)}) %all-gather.5.cloned.1.call-update) | async-done | bytes 3162128 | tf_op jit(solution)/shard_map/all_gather | solution.py:34
  109.6 2.6 fusion
  112.2 0.9 slice_convert_fusion.1
  113.1 6.0 %fusion.26 = bf16[192,384]{1,0:T(8,128)(2,1)S(1)} fusion(bf16[8192,384]{0,1:T(8,128)(2,1)} %bitcast.60, bf16[8192,384]{0,1:T(8,128)(2,1)} %collective-permute-done.2, pred[]{:T(512)S(6)} %eq.12, f32[8192]{0:T(1024)S(1)} %bitcast.65, f32[192]{0:T(256)S(1)} %add_rsqrt_fusion.1, bf16[193,8192]{1,0:T(8,128)(2,1)} %all-gather.5.cloned.1.call-done), kind=kOutput, calls=%fused_computation.32 | convolution fusion | flops 1217470464 | bytes 15909633 | tf_op jit(solution)/shard_map/dot_general | solution.py:39
  119.1 3.1 collective-permute-start.3
  122.3 3.0 collective-permute-start.4
  125.3 2.7 collective-permute-done.3
  128.1 2.7 collective-permute-done.4
  131.0 10.6 %while.32 = (s32[]{:T(128)}, f32[192,128]{1,0:T(8,128)S(1)}, f32[128,128]{1,0:T(8,128)S(1)}, f32[319,128]{1,0:T(8,128)S(1)}, s32[]{:T(128)}, /*index=5*/s32[]{:T(128)}, s32[]{:T(128)}, s32[]{:T(128)}) while((s32[]{:T(128)}, f32[192,128]{1,0:T(8,128)S(1)}, f32[128,128]{1,0:T(8,128)S(1)}, f32[319,128]{1,0:T(8,128)S(1)}, s32[]{:T(128)}, ...), condition=%wide.region_2.3_spmd.clone, body=%wide.region_1.2_spmd.clone.sunk | while | flops 73735 | bytes 296597 | solution.py:63
  142.4 2.9 copy.12
  145.8 4.0 collective-permute-done.5
  149.8 60.7 %all-gather.7.cloned.1.call-done = bf16[192,4096]{1,0:T(8,128)(2,1)} async-done(((bf16[192,128]{1,0:T(8,128)(2,1)}), bf16[192,4096]{1,0:T(8,128)(2,1)}) %all-gather.7.cloned.1.call-update) | async-done | bytes 1572880 | tf_op jit(solution)/shard_map/all_gather | solution.py:65
  210.5 2.0 fusion.39
  213.3 80.0 %all-gather.9.cloned.1.call-done = bf16[193,8192]{1,0:T(8,128)(2,1)} async-done(((bf16[193,256]{1,0:T(8,128)(2,1)}), bf16[193,8192]{1,0:T(8,128)(2,1)}) %all-gather.9.cloned.1.call-update) | async-done | bytes 3162128 | tf_op jit(solution)/shard_map/all_gather | solution.py:34
  293.3 2.6 fusion.3
  295.9 0.9 slice_convert_fusion
  296.8 6.0 %fusion.31 = bf16[192,384]{1,0:T(8,128)(2,1)S(1)} fusion(bf16[8192,384]{0,1:T(8,128)(2,1)} %bitcast.61, bf16[8192,384]{0,1:T(8,128)(2,1)} %collective-permute-done.2, pred[]{:T(512)S(6)} %eq.33, f32[8192]{0:T(1024)S(1)} %bitcast.66, f32[192]{0:T(256)S(1)} %add_rsqrt_fusion, bf16[193,8192]{1,0:T(8,128)(2,1)} %all-gather.9.cloned.1.call-done), kind=kOutput, calls=%fused_computation.33 | convolution fusion | flops 1217470464 | bytes 15909633 | tf_op jit(solution)/shard_map/dot_general | solution.py:39
  302.8 3.2 collective-permute-start.6
  306.1 3.1 collective-permute-start.7
  309.2 2.2 collective-permute-done.6
  311.5 2.7 collective-permute-done.7
  314.4 96.0 %while.33 = (s32[]{:T(128)}, f32[192,128]{1,0:T(8,128)S(1)}, f32[128,128]{1,0:T(8,128)}, f32[319,128]{1,0:T(8,128)S(1)}, s32[]{:T(128)}, /*index=5*/s32[]{:T(128)}, s32[]{:T(128)}, s32[]{:T(128)}) while((s32[]{:T(128)}, f32[192,128]{1,0:T(8,128)S(1)}, f32[128,128]{1,0:T(8,128)}, f32[319,128]{1,0:T(8,128)S(1)}, s32[]{:T(128)}, ...), condition=%wide.region_5.6_spmd.clone, body=%wide.region_4.5_spmd.clone.sunk | while | flops 73735 | bytes 296597 | solution.py:63
  314.4 0.7 dynamic-slice_bitcast_fusion.5
  315.2 0.7 dynamic-slice_bitcast_fusion.5
  315.9 0.7 dynamic-slice_bitcast_fusion.5
  316.7 0.7 dynamic-slice_bitcast_fusion.5
  317.4 0.7 dynamic-slice_bitcast_fusion.5
  318.2 0.7 dynamic-slice_bitcast_fusion.5
  318.9 0.7 dynamic-slice_bitcast_fusion.5
  319.7 0.7 dynamic-slice_bitcast_fusion.5
  320.4 0.7 dynamic-slice_bitcast_fusion.5
  321.2 0.7 dynamic-slice_bitcast_fusion.5
  321.9 0.7 dynamic-slice_bitcast_fusion.5
  322.7 0.7 dynamic-slice_bitcast_fusion.5
  323.4 0.7 dynamic-slice_bitcast_fusion.5
  324.2 0.7 dynamic-slice_bitcast_fusion.5
  324.9 0.7 dynamic-slice_bitcast_fusion.5
  325.7 0.7 dynamic-slice_bitcast_fusion.5
  326.4 0.7 dynamic-slice_bitcast_fusion.5
  327.2 0.7 dynamic-slice_bitcast_fusion.5
  327.9 0.7 dynamic-slice_bitcast_fusion.5
  328.7 0.7 dynamic-slice_bitcast_fusion.5
  329.4 0.7 dynamic-slice_bitcast_fusion.5
  330.2 0.7 dynamic-slice_bitcast_fusion.5
  330.9 0.7 dynamic-slice_bitcast_fusion.5
  331.7 0.7 dynamic-slice_bitcast_fusion.5
  332.4 0.7 dynamic-slice_bitcast_fusion.5
  333.2 0.7 dynamic-slice_bitcast_fusion.5
  333.9 0.7 dynamic-slice_bitcast_fusion.5
  334.7 0.7 dynamic-slice_bitcast_fusion.5
  335.4 0.7 dynamic-slice_bitcast_fusion.5
  336.2 0.7 dynamic-slice_bitcast_fusion.5
  336.9 0.7 dynamic-slice_bitcast_fusion.5
  411.1 2.5 collective-permute-start.9
  413.6 68.0 %all-gather.11.cloned.1.call-done = bf16[192,4096]{1,0:T(8,128)(2,1)} async-done(((bf16[192,128]{1,0:T(8,128)(2,1)}), bf16[192,4096]{1,0:T(8,128)(2,1)}) %all-gather.11.cloned.1.call-update) | async-done | bytes 1572880 | tf_op jit(solution)/shard_map/all_gather | solution.py:65
  481.6 2.0 fusion.20
  483.7 1.3 collective-permute-start.8
  485.0 5.4 %collective-permute-done.8 = bf16[192,256]{1,0:T(8,128)(2,1)S(1)} collective-permute-done((bf16[192,256]{1,0:T(8,128)(2,1)S(1)}, bf16[192,256]{1,0:T(8,128)(2,1)S(1)}, u32[]{:S(2)}, u32[]{:S(2)}) %collective-permute-start.8) | collective-permute-done | bytes 98336 | tf_op jit(solution)/shard_map/ppermute | solution.py:98
  490.5 0.7 maximum_bitcast_fusion
  (547 shorter events, 82.3 us)
Async XLA Ops:
  6.5 4.7 copy-start
  6.5 103.0 %all-gather.5.cloned.1.call-start = ((), (), s32[]{:S(2)}) async-start(), calls=%async_computation.1 | async-start | bytes 3379200 | tf_op jit(solution)/shard_map/all_gather | solution.py:34
  7.3 4.3 collective-permute-start.1
  12.3 9.0 %copy-start.3 = (f32[1,3,3,128]{3,0,2,1:T(1,128)S(1)}, f32[1,3,3,128]{3,0,2,1:T(1,128)}, u32[]{:S(2)}) copy-start(f32[1,3,3,128]{3,0,2,1:T(1,128)} %param.15) | copy-start | bytes 13828
  12.3 9.4 %copy-start.1 = (bf16[1,128,8192]{2,1,0:T(8,128)(2,1)S(1)}, bf16[1,128,8192]{2,1,0:T(8,128)(2,1)}, u32[]{:S(2)}) copy-start(bf16[1,128,8192]{2,1,0:T(8,128)(2,1)} %param.18) | copy-start | bytes 6291460
  21.1 92.0 %collective-permute-start.2 = (bf16[8192,384]{0,1:T(8,128)(2,1)}, bf16[8192,384]{0,1:T(8,128)(2,1)}, u32[]{:S(2)}, u32[]{:S(2)}) collective-permute-start(bf16[8192,384]{0,1:T(8,128)(2,1)} %bitcast.59), channel_id=1, source_target_pairs={{0,128},{128,0},{1,129},{129,1},{2,130},{130,2},{3,131},{131,3},{4... | collective-permute-start | bytes 18874376 | tf_op jit(solution)/shard_map/ppermute | solution.py:15
  21.3 12.4 %copy-start.4 = (f32[7,128]{1,0:T(8,128)S(1)}, f32[7,128]{1,0:T(8,128)}, u32[]{:S(2)}) copy-start(f32[7,128]{1,0:T(8,128)} %param.16) | copy-start | bytes 10756
  21.3 12.4 %collective-permute-start = (f32[3,3,128]{2,1,0:T(4,128)S(1)}, f32[3,3,128]{2,1,0:T(4,128)S(1)}, u32[]{:S(2)}, u32[]{:S(2)}) collective-permute-start(f32[3,3,128]{2,1,0:T(4,128)S(1)} %bitcast.67), channel_id=1, source_target_pairs={{0,128},{128,0},{1,129},{129,1},{2,130},{130,2},{3,131},{131,3},{4... | collective-permute-start | bytes 13832 | tf_op jit(solution)/shard_map/ppermute | solution.py:15
  24.1 118.2 %all-to-all-start = ((bf16[128,32,256]{0,2,1:T(8,128)(2,1)}), bf16[128,32,256]{0,2,1:T(8,128)(2,1)S(1)}, u32[]{:S(2)}, u32[]{:S(2)}) async-start(bf16[128,32,256]{0,2,1:T(8,128)(2,1)} %bitcast.58), calls=%async_computation | async-start | bytes 4194304 | tf_op jit(solution)/shard_map/all_to_all | solution.py:26
  33.6 176.9 %all-gather.7.cloned.1.call-start = ((), (), s32[]{:S(2)}) async-start(), calls=%async_computation.2 | async-start | bytes 1622016 | tf_op jit(solution)/shard_map/all_gather | solution.py:65
  119.1 8.9 %collective-permute-start.3 = (bf16[2,128]{1,0:T(2,128)(2,1)S(1)}, bf16[2,128]{1,0:T(2,128)(2,1)S(1)}, u32[]{:S(2)}, u32[]{:S(2)}) collective-permute-start(bf16[2,128]{1,0:T(2,128)(2,1)S(1)} %slice.191), channel_id=1, source_target_pairs={{0,32},{32,64},{64,96},{96,128},{128,160},{160,192},{192,224},{1,3... | collective-permute-start | bytes 1544 | tf_op jit(solution)/shard_map/ppermute | solution.py:43
  122.3 8.5 %collective-permute-start.4 = (bf16[129,256]{1,0:T(8,128)(2,1)S(1)}, bf16[129,256]{1,0:T(8,128)(2,1)S(1)}, u32[]{:S(2)}, u32[]{:S(2)}) collective-permute-start(bf16[129,256]{1,0:T(8,128)(2,1)S(1)} %slice.199), channel_id=1, source_target_pairs={{0,32},{32,64},{64,96},{96,128},{128,160},{160,192},{192,224},{1,3... | collective-permute-start | bytes 198152 | tf_op jit(solution)/shard_map/ppermute | solution.py:43
  142.3 151.0 %all-gather.9.cloned.1.call-start = ((), (), s32[]{:S(2)}) async-start(), calls=%async_computation.3 | async-start | bytes 3379200 | tf_op jit(solution)/shard_map/all_gather | solution.py:34
  145.3 4.5 collective-permute-start.5
  149.8 62.7 %copy-start.5 = (bf16[4096,256]{1,0:T(8,128)(2,1)}, bf16[4096,256]{1,0:T(8,128)(2,1)S(1)}, u32[]{:S(2)}) copy-start(bf16[4096,256]{1,0:T(8,128)(2,1)S(1)} %collective-permute-done.5) | copy-start | bytes 6291460
  213.2 268.4 %all-gather.11.cloned.1.call-start = ((), (), s32[]{:S(2)}) async-start(), calls=%async_computation.4 | async-start | bytes 1622016 | tf_op jit(solution)/shard_map/all_gather | solution.py:65
  302.8 178.8 %copy-start.2 = (bf16[32,128,1,256]{3,1,0,2:T(8,128)(2,1)S(1)}, bf16[32,128,1,256]{3,1,0,2:T(8,128)(2,1)}, u32[]{:S(2)}) copy-start(bf16[32,128,1,256]{3,1,0,2:T(8,128)(2,1)} %copy.12) | copy-start | bytes 6291460
  302.8 8.6 %collective-permute-start.6 = (bf16[2,128]{1,0:T(2,128)(2,1)S(1)}, bf16[2,128]{1,0:T(2,128)(2,1)S(1)}, u32[]{:S(2)}, u32[]{:S(2)}) collective-permute-start(bf16[2,128]{1,0:T(2,128)(2,1)S(1)} %slice.211), channel_id=1, source_target_pairs={{0,32},{32,64},{64,96},{96,128},{128,160},{160,192},{192,224},{1,3... | collective-permute-start | bytes 1544 | tf_op jit(solution)/shard_map/ppermute | solution.py:43
  306.1 8.1 %collective-permute-start.7 = (bf16[129,256]{1,0:T(8,128)(2,1)S(1)}, bf16[129,256]{1,0:T(8,128)(2,1)S(1)}, u32[]{:S(2)}, u32[]{:S(2)}) collective-permute-start(bf16[129,256]{1,0:T(8,128)(2,1)S(1)} %slice.219), channel_id=1, source_target_pairs={{0,32},{32,64},{64,96},{96,128},{128,160},{160,192},{192,224},{1,3... | collective-permute-start | bytes 198152 | tf_op jit(solution)/shard_map/ppermute | solution.py:43
  411.1 72.6 %collective-permute-start.9 = (bf16[192,256]{1,0:T(8,128)(2,1)S(1)}, bf16[192,256]{1,0:T(8,128)(2,1)S(1)}, u32[]{:S(2)}, u32[]{:S(2)}) collective-permute-start(bf16[192,256]{1,0:T(8,128)(2,1)S(1)} %fusion.39), channel_id=1, source_target_pairs={{128,0},{129,1},{130,2},{131,3},{132,4},{133,5},{134,6},{135,7},{1... | collective-permute-start | bytes 294920 | tf_op jit(solution)/shard_map/ppermute | solution.py:97
  483.7 6.7 %collective-permute-start.8 = (bf16[192,256]{1,0:T(8,128)(2,1)S(1)}, bf16[192,256]{1,0:T(8,128)(2,1)S(1)}, u32[]{:S(2)}, u32[]{:S(2)}) collective-permute-start(bf16[192,256]{1,0:T(8,128)(2,1)S(1)} %get-tuple-element.274), channel_id=1, source_target_pairs={{0,128},{1,129},{2,130},{3,131},{4,132},{5,133},{6,134},{7,135},{8... | collective-permute-start | bytes 294920 | tf_op jit(solution)/shard_map/ppermute | solution.py:98
Sparse Core Ops, SparseCore 0:
  12.4 97.1 all-gather.4
  142.4 68.0 all-gather.6
  213.3 79.9 all-gather.8
  411.2 70.3 all-gather.10
where the time goes:
time: 502 us; the launch traced here: 498 us
  waiting for transfers between devices  305 us (61%)
  local copies, waits for them, and re-layouts  105 us (21%)
  starting transfers between devices  30.1 us (6%)
  other arithmetic  19.8 us (4%)
  matrix products  16.2 us (3%)
  between operations  13.5 us (3%)
  loops' own time  8.15 us (2%)
    all_gather x2, waiting for transfers between devices, section_step(): full = lax.all_gather(aug, 'tensor', axis=1, tiled=True)  156 us
    all_gather x2, waiting for transfers between devices, section_step(): y_full = lax.all_gather(y_out, 'tensor', axis=1, tiled=True)  129 us
    mul x256, local copies, waits for them, and re-layouts, add_tap(): return running + long_taps[tap_index] * shifted  90.3 us
    ppermute x4, starting transfers between devices, section_step(): lax.ppermute((kv_tail, q_tail), ('pipe', 'seq'), [(b, b + 1) for b in ran...  12.4 us
    dot_general x2, matrix products, section_step(): jnp.dot(normed, w_in, preferred_element_type=jnp.float32)  12 us
    unnamed x15, local copies, waits for them, and re-layouts  11.3 us
    ppermute x4, waiting for transfers between devices, section_step(): lax.ppermute((kv_tail, q_tail), ('pipe', 'seq'), [(b, b + 1) for b in ran...  10.5 us
  transfers between devices with their start and end apart: 15, of which 10 were waited for; matrix products, arithmetic and copies ran while one was open for 7% of the time, Pallas kernels for 0%

commit v1 on v0

--- a/solution.py
+++ b/solution.py
@@ -9,6 +9,11 @@
 KF = 3
 HALO = KL + KF - 2
 epsilon = 1e-06
+
+
+def gather_by_exchange(x, axis, dim):
+    copies = jnp.concatenate([x] * lax.axis_size(axis), axis=dim)
+    return lax.all_to_all(copies, axis, dim, dim, tiled=True)
 
 
 def swapped(value):
@@ -62,7 +67,7 @@
 
     filtered = lax.fori_loop(0, KL, add_tap, jnp.zeros_like(q_feat))
     y_out = (q_feat * filtered).astype(jnp.bfloat16)
-    y_full = lax.all_gather(y_out, "tensor", axis=1, tiled=True)
+    y_full = gather_by_exchange(y_out, "tensor", 1)
     mixed = jnp.dot(y_full, w_out, preferred_element_type=jnp.float32)
     return (x_in.astype(jnp.float32) + mixed).astype(jnp.bfloat16)
 

time: 502 us -> 450 us (0.90)
  waiting for transfers between devices: 305 us -> 233 us
  starting transfers between devices: 30.1 us -> 46 us
    all_gather x2 -> x0, waiting for transfers between devices: 129 us -> none  [section_step(): y_full = lax.all_gather(y_out, 'tensor', axis=1, tiled=True)]
    all_to_all x0 -> x2, waiting for transfers between devices: none -> 65.1 us  [gather_by_exchange(): return lax.all_to_all(copies, axis, dim, dim, tiled=True)]
    all_to_all x0 -> x2, starting transfers between devices: none -> 15.3 us  [gather_by_exchange(): return lax.all_to_all(copies, axis, dim, dim, tiled=True)]
    all_gather x2, waiting for transfers between devices: 156 us -> 149 us  [section_step(): full = lax.all_gather(aug, 'tensor', axis=1, tiled=True)]
    unnamed x15 -> x75, local copies, waits for them, and re-layouts: 11.3 us -> 12.3 us
  transfers between devices with their start and end apart: 15 -> 15, of which waited for: 10 -> 10; matrix products, arithmetic and copies ran while one was open for 7% -> 8% of each run, Pallas kernels for 0% -> 0%
where the time goes in v1:
time: 450 us; the launch traced here: 445 us
  waiting for transfers between devices  233 us (52%)
  local copies, waits for them, and re-layouts  110 us (24%)
  starting transfers between devices  46 us (10%)
  other arithmetic  18.5 us (4%)
  matrix products  16.2 us (4%)
  between operations  14.2 us (3%)
  loops' own time  8.15 us (2%)
    all_gather x2, waiting for transfers between devices, section_step(): full = lax.all_gather(aug, 'tensor', axis=1, tiled=True)  149 us
    mul x256, local copies, waits for them, and re-layouts, add_tap(): return running + long_taps[tap_index] * shifted  90.3 us
    all_to_all x2, waiting for transfers between devices, gather_by_exchange(): return lax.all_to_all(copies, axis, dim, dim, tiled=True)  65.1 us
    all_to_all x2, starting transfers between devices, gather_by_exchange(): return lax.all_to_all(copies, axis, dim, dim, tiled=True)  15.3 us
    ppermute x4, starting transfers between devices, section_step(): lax.ppermute((kv_tail, q_tail), ('pipe', 'seq'), [(b, b + 1) for b in ran...  12.5 us
    unnamed x75, local copies, waits for them, and re-layouts  12.3 us
    dot_general x2, matrix products, section_step(): jnp.dot(normed, w_in, preferred_element_type=jnp.float32)  12 us
    ppermute x4, waiting for transfers between devices, section_step(): lax.ppermute((kv_tail, q_tail), ('pipe', 'seq'), [(b, b + 1) for b in ran...  10.4 us
  transfers between devices with their start and end apart: 15, of which 10 were waited for; matrix products, arithmetic and copies ran while one was open for 8% of the time, Pallas kernels for 0%

profile of v1, /device:TPU:1, one launch (start us, length us, event | category | flops | bytes accessed | tf_op | source)
XLA Modules:
  0.0 445.3 jit_solution(16418198322817154175)
XLA Ops:
  6.5 0.7 reduce
  7.3 3.3 collective-permute-start.1
  12.3 8.9 %copy.18 = bf16[1,8192,3,128]{1,3,2,0:T(8,128)(2,1)} copy(bf16[1,8192,3,128]{3,1,2,0:T(8,128)(2,1)} %param.14) | data formatting | bytes 12582912 | tf_op args[2]
  21.7 2.4 copy.21
  24.1 9.6 %all-to-all-start.1 = ((bf16[128,32,256]{0,2,1:T(8,128)(2,1)}), bf16[128,32,256]{0,2,1:T(8,128)(2,1)S(1)}, u32[]{:S(2)}, u32[]{:S(2)}) async-start(bf16[128,32,256]{0,2,1:T(8,128)(2,1)} %bitcast.84), calls=%async_computation.1 | async-start | bytes 4194304 | tf_op jit(solution)/shard_map/all_to_all | solution.py:31
  33.8 75.6 %all-gather.3.cloned.1.call-done = bf16[193,8192]{1,0:T(8,128)(2,1)} async-done(((bf16[193,256]{1,0:T(8,128)(2,1)}), bf16[193,8192]{1,0:T(8,128)(2,1)}) %all-gather.3.cloned.1.call-update) | async-done | bytes 3162128 | tf_op jit(solution)/shard_map/all_gather | solution.py:39
  109.4 2.6 fusion
  112.0 0.9 slice_convert_fusion.1
  112.9 6.0 %fusion.30 = bf16[192,384]{1,0:T(8,128)(2,1)S(1)} fusion(bf16[8192,384]{0,1:T(8,128)(2,1)} %bitcast.86, bf16[8192,384]{0,1:T(8,128)(2,1)} %collective-permute-done.2, pred[]{:T(512)S(6)} %eq.12, f32[8192]{0:T(1024)S(1)} %bitcast.91, f32[192]{0:T(256)S(1)} %add_rsqrt_fusion.1, bf16[193,8192]{1,0:T(8,128)(2,1)} %all-gather.3.cloned.1.call-done), kind=kOutput, calls=%fused_computation.38 | convolution fusion | flops 1217470464 | bytes 15909633 | tf_op jit(solution)/shard_map/dot_general | solution.py:44
  118.9 3.1 collective-permute-start.3
  122.1 3.2 collective-permute-start.4
  125.3 2.7 collective-permute-done.3
  128.1 2.7 collective-permute-done.4
  131.0 10.6 %while.32 = (s32[]{:T(128)}, f32[192,128]{1,0:T(8,128)S(1)}, f32[128,128]{1,0:T(8,128)S(1)}, f32[319,128]{1,0:T(8,128)S(1)}, s32[]{:T(128)}, /*index=5*/s32[]{:T(128)}, s32[]{:T(128)}, s32[]{:T(128)}) while((s32[]{:T(128)}, f32[192,128]{1,0:T(8,128)S(1)}, f32[128,128]{1,0:T(8,128)S(1)}, f32[319,128]{1,0:T(8,128)S(1)}, s32[]{:T(128)}, ...), condition=%wide.region_2.3_spmd.clone, body=%wide.region_1.2_spmd.clone.sunk | while | flops 73735 | bytes 296597 | solution.py:68
  142.4 1.6 copy_bitcast_fusion.1
  144.0 6.3 %all-to-all-start = ((bf16[192,32,128]{2,0,1:T(8,128)(2,1)}), bf16[192,32,128]{2,0,1:T(8,128)(2,1)}, u32[]{:S(2)}, u32[]{:S(2)}) async-start(bf16[192,32,128]{2,0,1:T(8,128)(2,1)} %copy_bitcast_fusion.1), calls=%async_computation | async-start | bytes 3145728 | tf_op jit(solution)/shard_map/all_to_all | solution.py:16
  150.3 2.9 copy.22
  153.9 4.0 collective-permute-done.5
  157.9 30.1 %all-to-all-done = bf16[192,32,128]{2,0,1:T(8,128)(2,1)} async-done(((bf16[192,32,128]{2,0,1:T(8,128)(2,1)}), bf16[192,32,128]{2,0,1:T(8,128)(2,1)}, u32[]{:S(2)}, u32[]{:S(2)}) %all-to-all-start) | async-done | bytes 1572896 | tf_op jit(solution)/shard_map/all_to_all | solution.py:16
  188.0 2.0 fusion.45
  190.7 73.9 %all-gather.5.cloned.1.call-done = bf16[193,8192]{1,0:T(8,128)(2,1)} async-done(((bf16[193,256]{1,0:T(8,128)(2,1)}), bf16[193,8192]{1,0:T(8,128)(2,1)}) %all-gather.5.cloned.1.call-update) | async-done | bytes 3162128 | tf_op jit(solution)/shard_map/all_gather | solution.py:39
  264.6 2.6 fusion.3
  267.2 0.9 slice_convert_fusion
  268.1 6.0 %fusion.35 = bf16[192,384]{1,0:T(8,128)(2,1)S(1)} fusion(bf16[8192,384]{0,1:T(8,128)(2,1)} %bitcast.87, bf16[8192,384]{0,1:T(8,128)(2,1)} %collective-permute-done.2, pred[]{:T(512)S(6)} %eq.33, f32[8192]{0:T(1024)S(1)} %bitcast.92, f32[192]{0:T(256)S(1)} %add_rsqrt_fusion, bf16[193,8192]{1,0:T(8,128)(2,1)} %all-gather.5.cloned.1.call-done), kind=kOutput, calls=%fused_computation.39 | convolution fusion | flops 1217470464 | bytes 15909633 | tf_op jit(solution)/shard_map/dot_general | solution.py:44
  274.1 3.1 collective-permute-start.6
  277.3 3.1 collective-permute-start.7
  280.4 2.2 collective-permute-done.6
  282.7 2.7 collective-permute-done.7
  285.6 96.0 %while.33 = (s32[]{:T(128)}, f32[192,128]{1,0:T(8,128)S(1)}, f32[128,128]{1,0:T(8,128)}, f32[319,128]{1,0:T(8,128)S(1)}, s32[]{:T(128)}, /*index=5*/s32[]{:T(128)}, s32[]{:T(128)}, s32[]{:T(128)}) while((s32[]{:T(128)}, f32[192,128]{1,0:T(8,128)S(1)}, f32[128,128]{1,0:T(8,128)}, f32[319,128]{1,0:T(8,128)S(1)}, s32[]{:T(128)}, ...), condition=%wide.region_5.6_spmd.clone, body=%wide.region_4.5_spmd.clone.sunk | while | flops 73735 | bytes 296597 | solution.py:68
  285.6 0.7 dynamic-slice_bitcast_fusion.5
  286.3 0.7 dynamic-slice_bitcast_fusion.5
  287.1 0.7 dynamic-slice_bitcast_fusion.5
  287.8 0.7 dynamic-slice_bitcast_fusion.5
  288.6 0.7 dynamic-slice_bitcast_fusion.5
  289.3 0.7 dynamic-slice_bitcast_fusion.5
  290.1 0.7 dynamic-slice_bitcast_fusion.5
  290.8 0.7 dynamic-slice_bitcast_fusion.5
  291.6 0.7 dynamic-slice_bitcast_fusion.5
  292.3 0.7 dynamic-slice_bitcast_fusion.5
  293.1 0.7 dynamic-slice_bitcast_fusion.5
  293.8 0.7 dynamic-slice_bitcast_fusion.5
  294.6 0.7 dynamic-slice_bitcast_fusion.5
  295.3 0.7 dynamic-slice_bitcast_fusion.5
  296.1 0.7 dynamic-slice_bitcast_fusion.5
  296.8 0.7 dynamic-slice_bitcast_fusion.5
  297.6 0.7 dynamic-slice_bitcast_fusion.5
  298.3 0.7 dynamic-slice_bitcast_fusion.5
  299.1 0.7 dynamic-slice_bitcast_fusion.5
  299.8 0.7 dynamic-slice_bitcast_fusion.5
  300.6 0.7 dynamic-slice_bitcast_fusion.5
  301.3 0.7 dynamic-slice_bitcast_fusion.5
  302.1 0.7 dynamic-slice_bitcast_fusion.5
  302.8 0.7 dynamic-slice_bitcast_fusion.5
  303.6 0.7 dynamic-slice_bitcast_fusion.5
  304.3 0.7 dynamic-slice_bitcast_fusion.5
  305.1 0.7 dynamic-slice_bitcast_fusion.5
  305.8 0.7 dynamic-slice_bitcast_fusion.5
  382.3 1.6 copy_bitcast_fusion
  383.9 9.0 %all-to-all-start.2 = ((bf16[192,32,128]{2,0,1:T(8,128)(2,1)}), bf16[192,32,128]{2,0,1:T(8,128)(2,1)}, u32[]{:S(2)}, u32[]{:S(2)}) async-start(bf16[192,32,128]{2,0,1:T(8,128)(2,1)} %copy_bitcast_fusion), calls=%async_computation.2 | async-start | bytes 3145728 | tf_op jit(solution)/shard_map/all_to_all | solution.py:16
  392.9 2.8 collective-permute-start.9
  395.7 35.0 %all-to-all-done.2 = bf16[192,32,128]{2,0,1:T(8,128)(2,1)} async-done(((bf16[192,32,128]{2,0,1:T(8,128)(2,1)}), bf16[192,32,128]{2,0,1:T(8,128)(2,1)}, u32[]{:S(2)}, u32[]{:S(2)}) %all-to-all-start.2) | async-done | bytes 1572896 | tf_op jit(solution)/shard_map/all_to_all | solution.py:16
  430.6 2.0 fusion.20
  432.7 1.3 collective-permute-start.8
  434.0 3.8 collective-permute-done.8
  (609 shorter events, 84.9 us)
Async XLA Ops:
  6.5 4.7 %copy-start = (bf16[512,256]{1,0:T(8,128)(2,1)S(1)}, bf16[512,256]{1,0:T(8,128)(2,1)}, u32[]{:S(2)}) copy-start(bf16[512,256]{1,0:T(8,128)(2,1)} %param.13) | copy-start | bytes 786436
  6.5 102.8 %all-gather.3.cloned.1.call-start = ((), (), s32[]{:S(2)}) async-start(), calls=%async_computation.3 | async-start | bytes 3379200 | tf_op jit(solution)/shard_map/all_gather | solution.py:39
  7.3 4.3 collective-permute-start.1
  12.3 9.0 %copy-start.3 = (f32[1,3,3,128]{3,0,2,1:T(1,128)S(1)}, f32[1,3,3,128]{3,0,2,1:T(1,128)}, u32[]{:S(2)}) copy-start(f32[1,3,3,128]{3,0,2,1:T(1,128)} %param.15) | copy-start | bytes 13828
  12.3 9.4 %copy-start.1 = (bf16[1,128,8192]{2,1,0:T(8,128)(2,1)S(1)}, bf16[1,128,8192]{2,1,0:T(8,128)(2,1)}, u32[]{:S(2)}) copy-start(bf16[1,128,8192]{2,1,0:T(8,128)(2,1)} %param.18) | copy-start | bytes 6291460
  21.1 91.8 %collective-permute-start.2 = (bf16[8192,384]{0,1:T(8,128)(2,1)}, bf16[8192,384]{0,1:T(8,128)(2,1)}, u32[]{:S(2)}, u32[]{:S(2)}) collective-permute-start(bf16[8192,384]{0,1:T(8,128)(2,1)} %bitcast.85), channel_id=1, source_target_pairs={{0,128},{128,0},{1,129},{129,1},{2,130},{130,2},{3,131},{131,3},{4... | collective-permute-start | bytes 18874376 | tf_op jit(solution)/shard_map/ppermute | solution.py:20
  21.3 12.5 %collective-permute-start = (f32[3,3,128]{2,1,0:T(4,128)S(1)}, f32[3,3,128]{2,1,0:T(4,128)S(1)}, u32[]{:S(2)}, u32[]{:S(2)}) collective-permute-start(f32[3,3,128]{2,1,0:T(4,128)S(1)} %bitcast.93), channel_id=1, source_target_pairs={{0,128},{128,0},{1,129},{129,1},{2,130},{130,2},{3,131},{131,3},{4... | collective-permute-start | bytes 13832 | tf_op jit(solution)/shard_map/ppermute | solution.py:20
  24.1 9.6 %copy-start.4 = (f32[7,128]{1,0:T(8,128)S(1)}, f32[7,128]{1,0:T(8,128)}, u32[]{:S(2)}) copy-start(f32[7,128]{1,0:T(8,128)} %param.16) | copy-start | bytes 10756
  24.1 119.9 %all-to-all-start.1 = ((bf16[128,32,256]{0,2,1:T(8,128)(2,1)}), bf16[128,32,256]{0,2,1:T(8,128)(2,1)S(1)}, u32[]{:S(2)}, u32[]{:S(2)}) async-start(bf16[128,32,256]{0,2,1:T(8,128)(2,1)} %bitcast.84), calls=%async_computation.1 | async-start | bytes 4194304 | tf_op jit(solution)/shard_map/all_to_all | solution.py:31
  118.9 9.1 %collective-permute-start.3 = (bf16[2,128]{1,0:T(2,128)(2,1)S(1)}, bf16[2,128]{1,0:T(2,128)(2,1)S(1)}, u32[]{:S(2)}, u32[]{:S(2)}) collective-permute-start(bf16[2,128]{1,0:T(2,128)(2,1)S(1)} %slice.191), channel_id=1, source_target_pairs={{0,32},{32,64},{64,96},{96,128},{128,160},{160,192},{192,224},{1,3... | collective-permute-start | bytes 1544 | tf_op jit(solution)/shard_map/ppermute | solution.py:48
  122.1 8.7 %collective-permute-start.4 = (bf16[129,256]{1,0:T(8,128)(2,1)S(1)}, bf16[129,256]{1,0:T(8,128)(2,1)S(1)}, u32[]{:S(2)}, u32[]{:S(2)}) collective-permute-start(bf16[129,256]{1,0:T(8,128)(2,1)S(1)} %slice.199), channel_id=1, source_target_pairs={{0,32},{32,64},{64,96},{96,128},{128,160},{160,192},{192,224},{1,3... | collective-permute-start | bytes 198152 | tf_op jit(solution)/shard_map/ppermute | solution.py:48
  144.0 44.1 %all-to-all-start = ((bf16[192,32,128]{2,0,1:T(8,128)(2,1)}), bf16[192,32,128]{2,0,1:T(8,128)(2,1)}, u32[]{:S(2)}, u32[]{:S(2)}) async-start(bf16[192,32,128]{2,0,1:T(8,128)(2,1)} %copy_bitcast_fusion.1), calls=%async_computation | async-start | bytes 3145728 | tf_op jit(solution)/shard_map/all_to_all | solution.py:16
  150.3 114.3 %all-gather.5.cloned.1.call-start = ((), (), s32[]{:S(2)}) async-start(), calls=%async_computation.4 | async-start | bytes 3379200 | tf_op jit(solution)/shard_map/all_gather | solution.py:39
  153.3 4.7 %collective-permute-start.5 = (bf16[4096,256]{1,0:T(8,128)(2,1)}, bf16[4096,256]{1,0:T(8,128)(2,1)S(1)}, u32[]{:S(2)}, u32[]{:S(2)}) collective-permute-start(bf16[4096,256]{1,0:T(8,128)(2,1)} %bitcast.88), channel_id=1, source_target_pairs={{0,128},{128,0},{1,129},{129,1},{2,130},{130,2},{3,131},{131,3},{4... | collective-permute-start | bytes 6291464 | tf_op jit(solution)/shard_map/ppermute | solution.py:20
  157.9 32.1 %copy-start.5 = (bf16[4096,256]{1,0:T(8,128)(2,1)}, bf16[4096,256]{1,0:T(8,128)(2,1)S(1)}, u32[]{:S(2)}) copy-start(bf16[4096,256]{1,0:T(8,128)(2,1)S(1)} %collective-permute-done.5) | copy-start | bytes 6291460
  274.1 8.5 %collective-permute-start.6 = (bf16[2,128]{1,0:T(2,128)(2,1)S(1)}, bf16[2,128]{1,0:T(2,128)(2,1)S(1)}, u32[]{:S(2)}, u32[]{:S(2)}) collective-permute-start(bf16[2,128]{1,0:T(2,128)(2,1)S(1)} %slice.211), channel_id=1, source_target_pairs={{0,32},{32,64},{64,96},{96,128},{128,160},{160,192},{192,224},{1,3... | collective-permute-start | bytes 1544 | tf_op jit(solution)/shard_map/ppermute | solution.py:48
  277.3 8.1 %collective-permute-start.7 = (bf16[129,256]{1,0:T(8,128)(2,1)S(1)}, bf16[129,256]{1,0:T(8,128)(2,1)S(1)}, u32[]{:S(2)}, u32[]{:S(2)}) collective-permute-start(bf16[129,256]{1,0:T(8,128)(2,1)S(1)} %slice.219), channel_id=1, source_target_pairs={{0,32},{32,64},{64,96},{96,128},{128,160},{160,192},{192,224},{1,3... | collective-permute-start | bytes 198152 | tf_op jit(solution)/shard_map/ppermute | solution.py:48
  383.9 46.7 %copy-start.2 = (bf16[32,128,1,256]{3,1,0,2:T(8,128)(2,1)S(1)}, bf16[32,128,1,256]{3,1,0,2:T(8,128)(2,1)}, u32[]{:S(2)}) copy-start(bf16[32,128,1,256]{3,1,0,2:T(8,128)(2,1)} %copy.22) | copy-start | bytes 6291460
  383.9 46.7 %all-to-all-start.2 = ((bf16[192,32,128]{2,0,1:T(8,128)(2,1)}), bf16[192,32,128]{2,0,1:T(8,128)(2,1)}, u32[]{:S(2)}, u32[]{:S(2)}) async-start(bf16[192,32,128]{2,0,1:T(8,128)(2,1)} %copy_bitcast_fusion), calls=%async_computation.2 | async-start | bytes 3145728 | tf_op jit(solution)/shard_map/all_to_all | solution.py:16
  392.9 39.7 %collective-permute-start.9 = (bf16[192,256]{1,0:T(8,128)(2,1)S(1)}, bf16[192,256]{1,0:T(8,128)(2,1)S(1)}, u32[]{:S(2)}, u32[]{:S(2)}) collective-permute-start(bf16[192,256]{1,0:T(8,128)(2,1)S(1)} %fusion.45), channel_id=1, source_target_pairs={{128,0},{129,1},{130,2},{131,3},{132,4},{133,5},{134,6},{135,7},{1... | collective-permute-start | bytes 294920 | tf_op jit(solution)/shard_map/ppermute | solution.py:102
  432.7 5.1 %collective-permute-start.8 = (bf16[192,256]{1,0:T(8,128)(2,1)S(1)}, bf16[192,256]{1,0:T(8,128)(2,1)S(1)}, u32[]{:S(2)}, u32[]{:S(2)}) collective-permute-start(bf16[192,256]{1,0:T(8,128)(2,1)S(1)} %get-tuple-element.274), channel_id=1, source_target_pairs={{0,128},{1,129},{2,130},{3,131},{4,132},{5,133},{6,134},{7,135},{8... | collective-permute-start | bytes 294920 | tf_op jit(solution)/shard_map/ppermute | solution.py:103
Sparse Core Ops, SparseCore 0:
  12.4 96.9 all-gather.2
  190.8 73.7 all-gather.4
